TPU v7x, 512 devices: a whole 4x8x8 slice. The times are simulated.
512 devices in a mesh: nodes: 128 (over z, y, core), rep: 4 (over x).
Axes of the slice: x: 4, y: 8, z: 8, core: 2. Of those that a mesh axis runs over, the one named last changes fastest.
Arguments:
- memory: float32 [65536, 512], P('nodes'), may hold values from -16 to 16
- last_tick: int32 [65536], P('nodes'), may hold values from 0 to 499
- src_local: int32 [65536], P(('nodes', 'rep')), may hold values from 0 to 511
- dst_owner: int32 [65536, 1], P(('nodes', 'rep')), may hold values from 0 to 127; in each aligned block of 128 rows (0 to 127, 128 to 255, ...) at most 2 rows name the same one
- dst_local: int32 [65536], P(('nodes', 'rep')), may hold values from 0 to 511
- event_tick: int32 [65536], P(('nodes', 'rep')), may hold values from 500 to 999
- nbr_owner: int32 [65536, 16, 1], P(('nodes', 'rep')), may hold values from 0 to 127; in each aligned block of 2048 rows (0 to 2047, 2048 to 4095, ..., all dimensions but the last counted through in order) at most 32 rows name the same one
- nbr_local: int32 [65536, 16], P(('nodes', 'rep')), may hold values from 0 to 511
- nbr_tick: int32 [65536, 16], P(('nodes', 'rep')), may hold values from 0 to 499
- freq: float32 [128], replicated, may hold values from 0.002 to 0.5
- phase: float32 [128], replicated, may hold values from -3.140625 to 3.140625
- w_message: bfloat16 [1152, 512], replicated, may hold values from -0.1875 to 0.1875
- gru_input: float32 [3, 512, 512], P(None, None, 'rep'), may hold values from -0.5 to 0.5
- gru_hidden: float32 [3, 512, 512], P(None, None, 'rep'), may hold values from -0.25 to 0.25
- gru_bias: float32 [4, 512], P(None, 'rep'), may hold values from -3 to 3
- w_query: bfloat16 [512, 512], replicated, may hold values from -1 to 1
- w_keyval_mem: bfloat16 [512, 1024], replicated, may hold values from -0.25 to 0.25
- w_keyval_time: bfloat16 [128, 1024], replicated, may hold values from -0.5 to 0.5
Outputs:
- new_memory: float32 [65536, 512], P('nodes', 'rep')
- embed: bfloat16 [65536, 512], P(('nodes', 'rep'))
Inputs may be any that keep to these rules, and one draw needn't show every extreme that they name: `dst_owner`: on one device no owner is named by more than 2 events. `nbr_owner`: on one device no owner is named by more than 32 neighbour entries.
All inputs are finite; a program needn't handle non-finite values.
Results may differ from a plain program's by a relative error of at most 0.012.
The roundings to bfloat16 on the way count: a program that leaves them out, or rounds other values in their place, can miss the bound.
Values may be sent and summed in bfloat16 or wider, within the bound.
No kernel may reach another device: no remote copies, remote signals or barrier semaphores. Data moves between devices by JAX's collectives and lax.ppermute only.
A program may use at most 128 MiB of HBM per device.

v0:
```python
import math
import jax
import jax.numpy as jnp
from jax import lax
from jax.sharding import PartitionSpec as P

HEADS = 8
HEAD_DIM = 64


def encode(gaps, freq, phase):
    return jnp.cos(gaps[..., None] * freq + phase)


def place(owner, groups, capacity):
    onehot = (owner[:, None] == jnp.arange(groups, dtype=jnp.int32)[None, :]).astype(jnp.int32)
    before = jnp.cumsum(onehot, axis=0) - onehot
    return owner * capacity + jnp.sum(before * onehot, axis=1)


def message_pair(src_rows, dst_rows, src_time, dst_time, w_message):
    count = src_rows.shape[0]
    stacked = jnp.concatenate(
        [
            jnp.concatenate([src_rows, dst_rows, src_time], axis=1),
            jnp.concatenate([dst_rows, src_rows, dst_time], axis=1),
        ],
        axis=0,
    )
    messages = jax.nn.silu(jnp.dot(stacked, w_message, preferred_element_type=jnp.float32)).astype(
        jnp.bfloat16
    )
    return (messages[:count], messages[count:])


def on_device(
    memory,
    last_tick,
    src_local,
    dst_owner,
    dst_local,
    event_tick,
    nbr_owner,
    nbr_local,
    nbr_tick,
    freq,
    phase,
    w_message,
    gru_input,
    gru_hidden,
    gru_bias,
    w_query,
    w_keyval_mem,
    w_keyval_time,
):
    groups = lax.axis_size("nodes")
    events = src_local.shape[0]
    rows_here = memory.shape[0]
    width_m = memory.shape[1]
    neighbours = nbr_local.shape[1]
    msg_width = w_message.shape[1]
    dst_cap = max(2, 2 * events // groups)
    nbr_cap = 2 * events * neighbours // groups
    dst_slot = place(dst_owner[:, 0], groups, dst_cap)
    nbr_slot = place(nbr_owner.reshape(-1), groups, nbr_cap)
    dst_ids = (
        jnp.full((groups * dst_cap,), -1, jnp.int32)
        .at[dst_slot]
        .set(dst_local)
        .reshape(groups, dst_cap)
    )
    nbr_ids = (
        jnp.full((groups * nbr_cap,), -1, jnp.int32)
        .at[nbr_slot]
        .set(nbr_local.reshape(-1))
        .reshape(groups, nbr_cap)
    )
    mem_half = memory.astype(jnp.bfloat16)
    near_rows = mem_half[src_local]
    near_ticks = last_tick[src_local]
    ticks = event_tick.astype(jnp.float32)
    got_dst, got_nbr = (
        lax.all_to_all(dst_ids, "nodes", split_axis=0, concat_axis=0, tiled=True),
        lax.all_to_all(nbr_ids, "nodes", split_axis=0, concat_axis=0, tiled=True),
    )
    safe_dst = jnp.maximum(got_dst, 0)
    reply_rows, reply_ticks = (
        lax.all_to_all(mem_half[safe_dst], "nodes", split_axis=0, concat_axis=0, tiled=True),
        lax.all_to_all(last_tick[safe_dst], "nodes", split_axis=0, concat_axis=0, tiled=True),
    )
    far_rows = reply_rows.reshape(-1, width_m)[dst_slot]
    far_ticks = reply_ticks.reshape(-1)[dst_slot]
    src_time = encode(ticks - near_ticks.astype(jnp.float32), freq, phase).astype(jnp.bfloat16)
    dst_time = encode(ticks - far_ticks.astype(jnp.float32), freq, phase).astype(jnp.bfloat16)
    msg_src, msg_dst = message_pair(near_rows, far_rows, src_time, dst_time, w_message)
    outgoing = (
        jnp.zeros((groups * dst_cap, msg_width), jnp.bfloat16)
        .at[dst_slot]
        .set(msg_dst)
        .reshape(groups, dst_cap, msg_width)
    )
    incoming = lax.all_to_all(outgoing, "nodes", split_axis=0, concat_axis=0, tiled=True)
    far_msgs = incoming.reshape(-1, msg_width)
    row_ids = jnp.arange(rows_here, dtype=jnp.int32)[:, None]
    hit_far = (row_ids == got_dst.reshape(1, -1)).astype(jnp.bfloat16)
    hit_near = (row_ids == src_local[None, :]).astype(jnp.bfloat16)
    sums = jnp.dot(hit_near, msg_src, preferred_element_type=jnp.float32) + jnp.dot(
        hit_far, far_msgs, preferred_element_type=jnp.float32
    )
    counts = jnp.sum(hit_near.astype(jnp.float32), axis=1) + jnp.sum(
        hit_far.astype(jnp.float32), axis=1
    )
    sums, counts = lax.psum((sums, counts), "rep")
    unit_width = gru_bias.shape[1]
    start = lax.axis_index("rep") * unit_width
    state_part = lax.dynamic_slice_in_dim(memory, start, unit_width, 1)
    mean = sums / jnp.maximum(counts, 1.0)[:, None]
    highest = lax.Precision.HIGHEST
    a_parts = jnp.einsum("rk,gku->gru", mean, gru_input, precision=highest)
    b_parts = jnp.einsum("rk,gku->gru", memory, gru_hidden, precision=highest)
    update = jax.nn.sigmoid(a_parts[0] + b_parts[0] + gru_bias[0])
    reset = jax.nn.sigmoid(a_parts[1] + b_parts[1] + gru_bias[1])
    cand = jnp.tanh(a_parts[2] + gru_bias[2] + reset * (b_parts[2] + gru_bias[3]))
    fresh = (1.0 - update) * cand + update * state_part
    new_part = jnp.where((counts > 0.0)[:, None], fresh, state_part)
    updated = lax.all_gather(new_part.astype(jnp.bfloat16), "rep", axis=1, tiled=True)
    served = updated[jnp.maximum(got_nbr, 0)]
    returned = lax.all_to_all(served, "nodes", split_axis=0, concat_axis=0, tiled=True)
    fetched = returned.reshape(-1, updated.shape[1])[nbr_slot]
    kv_mem = jnp.dot(fetched, w_keyval_mem, preferred_element_type=jnp.float32).astype(jnp.bfloat16)
    kv_mem = lax.optimization_barrier(kv_mem).astype(jnp.float32)
    gaps = ticks[:, None] - nbr_tick.astype(jnp.float32)
    time_enc = encode(gaps, freq, phase).reshape(-1, freq.shape[0]).astype(jnp.bfloat16)
    kv_time = jnp.dot(time_enc, w_keyval_time, preferred_element_type=jnp.float32)
    keyval = (kv_mem + kv_time).reshape(events, neighbours, 2, HEADS, HEAD_DIM)
    query = jnp.dot(updated[src_local], w_query, preferred_element_type=jnp.float32).astype(
        jnp.bfloat16
    )
    query = lax.optimization_barrier(query).astype(jnp.float32).reshape(events, HEADS, HEAD_DIM)
    scores = jnp.einsum("ehd,ejhd->ehj", query, keyval[:, :, 0]) / math.sqrt(HEAD_DIM)
    weights = jax.nn.softmax(scores, axis=-1)
    mixed = jnp.einsum("ehj,ejhd->ehd", weights, keyval[:, :, 1])
    embed = mixed.reshape(events, HEADS * HEAD_DIM).astype(jnp.bfloat16)
    return (new_part, embed)


def solution(mesh):
    placed = (
        P("nodes", None),
        P("nodes"),
        P(("nodes", "rep")),
        P(("nodes", "rep"), None),
        P(("nodes", "rep")),
        P(("nodes", "rep")),
        P(("nodes", "rep"), None, None),
        P(("nodes", "rep"), None),
        P(("nodes", "rep"), None),
        P(),
        P(),
        P(),
        P(None, None, "rep"),
        P(None, None, "rep"),
        P(None, "rep"),
        P(),
        P(),
        P(),
    )
    return jax.shard_map(
        on_device,
        mesh=mesh,
        in_specs=placed,
        out_specs=(P("nodes", "rep"), P(("nodes", "rep"), None)),
        check_vma=False,
    )
```

profile of v0, /device:TPU:41, one launch (start us, length us, event | category | flops | bytes accessed | tf_op | source)
XLA Modules:
  0.0 390.3 jit_solution(18406961669935850036)
XLA Ops:
  11.6 17.2 %all-to-all-start = ((s32[128,1,2]{2,1,0:T(1,128)}), s32[128,1,2]{2,1,0:T(1,128)S(1)}, u32[]{:S(2)}, u32[]{:S(2)}) async-start(s32[128,1,2]{2,1,0:T(1,128)} %bitcast.5), calls=%async_computation | async-start | bytes 131072 | tf_op jit(solution)/shard_map/all_to_all | solution.py:83
  32.7 4.2 %all-to-all-done = s32[128,1,2]{2,1,0:T(1,128)S(1)} async-done(((s32[128,1,2]{2,1,0:T(1,128)}), s32[128,1,2]{2,1,0:T(1,128)S(1)}, u32[]{:S(2)}, u32[]{:S(2)}) %all-to-all-start) | async-done | bytes 1056 | tf_op jit(solution)/shard_map/all_to_all | solution.py:83
  41.8 9.6 %all-to-all-start.2 = ((s32[128,1,2]{2,1,0:T(1,128)}), s32[128,1,2]{2,1,0:T(1,128)S(1)}, u32[]{:S(2)}, u32[]{:S(2)}) async-start(s32[128,1,2]{2,1,0:T(1,128)} %bitcast.6), calls=%async_computation.2 | async-start | bytes 131072 | tf_op jit(solution)/shard_map/all_to_all | solution.py:89
  56.0 3.5 all-to-all-done.2
  59.5 10.2 %all-to-all-start.1 = ((bf16[128,2,512]{2,1,0:T(2,128)(2,1)}), bf16[128,2,512]{2,1,0:T(2,128)(2,1)S(1)}, u32[]{:S(2)}, u32[]{:S(2)}) async-start(bf16[128,2,512]{2,1,0:T(2,128)(2,1)} %reshape.151), calls=%async_computation.1 | async-start | bytes 524288 | tf_op jit(solution)/shard_map/all_to_all | solution.py:88
  72.5 9.4 %all-to-all-done.1 = bf16[128,2,512]{2,1,0:T(2,128)(2,1)S(1)} async-done(((bf16[128,2,512]{2,1,0:T(2,128)(2,1)}), bf16[128,2,512]{2,1,0:T(2,128)(2,1)S(1)}, u32[]{:S(2)}, u32[]{:S(2)}) %all-to-all-start.1) | async-done | bytes 262176 | tf_op jit(solution)/shard_map/all_to_all | solution.py:88
  85.4 8.8 %all-to-all-start.3 = ((bf16[128,2,512]{2,1,0:T(2,128)(2,1)}), bf16[128,2,512]{2,1,0:T(2,128)(2,1)S(1)}, u32[]{:S(2)}, u32[]{:S(2)}) async-start(bf16[128,2,512]{2,1,0:T(2,128)(2,1)} %reshape.135), calls=%async_computation.3 | async-start | bytes 524288 | tf_op jit(solution)/shard_map/all_to_all | solution.py:102
  94.3 8.1 %scatter_custom_fusion.2 = s32[4096]{0:T(1024)S(1)} fusion(s32[2048]{0:T(1024)S(1)} %bitcast.137, s32[2048]{0:T(1024)S(1)} %reshape.234, s32[]{:T(128)} %constant.15.clone.1), kind=kCustom, calls=%fused_computation.109 | custom fusion | bytes 16388 | tf_op jit(solution)/shard_map/scatter | solution.py:75
  103.0 3.0 convolution_bitcast_fusion
  107.0 14.2 %all-to-all-start.4 = ((s32[128,1,32]{2,1,0:T(1,128)}), s32[128,1,32]{2,1,0:T(1,128)}, u32[]{:S(2)}, u32[]{:S(2)}) async-start(s32[128,1,32]{2,1,0:T(1,128)} %bitcast.135), calls=%async_computation.4 | async-start | bytes 131072 | tf_op jit(solution)/shard_map/all_to_all | solution.py:84
  121.7 2.2 convolution_add_fusion
  124.3 8.7 %psum.14 = f32[512]{0:T(512)S(1)} all-reduce(f32[512]{0:T(512)S(1)} %add.150), channel_id=1, replica_groups=mesh['nodes'=128,'rep'=4] {'rep'}, use_global_device_ids=true, to_apply=%region_5.6 | all-reduce | flops 512 | bytes 4096 | tf_op jit(solution)/shard_map/psum | solution.py:113
  134.1 46.1 %all-reduce.2.cloned.1.call-done = f32[512,512]{1,0:T(8,128)} async-done(((f32[512,512]{1,0:T(8,128)}), f32[512,512]{1,0:T(8,128)}) %all-reduce.2.cloned.1.call-update) | async-done | bytes 1048592 | tf_op jit(solution)/shard_map/psum | solution.py:113
  180.2 3.3 convolution_bitcast_fusion.1
  184.4 11.5 %all_gather.3 = bf16[512,512]{1,0:T(8,128)(2,1)S(1)} all-gather(bf16[512,128]{1,0:T(8,128)(2,1)S(1)} %get-tuple-element.10), channel_id=1, replica_groups=mesh['nodes'=128,'rep'=4] {'rep'}, dimensions={1}, use_global_device_ids=true | all-gather | bytes 655360 | tf_op jit(solution)/shard_map/all_gather | solution.py:126
  196.0 17.3 %gather_fusion.7 = bf16[4096,512]{1,0:T(8,128)(2,1)} fusion(bf16[512,512]{1,0:T(8,128)(2,1)S(1)} %all_gather.3, s32[4096]{0:T(1024)S(1)} %broadcast_clamp_fusion), kind=kCustom, calls=%fused_computation.7 | custom fusion | bytes 8404992 | tf_op jit(solution)/shard_map/gather | solution.py:127
  213.3 19.2 %all-to-all-start.5 = ((bf16[128,32,512]{2,1,0:T(8,128)(2,1)}), bf16[128,32,512]{2,1,0:T(8,128)(2,1)}, u32[]{:S(2)}, u32[]{:S(2)}) async-start(bf16[128,32,512]{2,1,0:T(8,128)(2,1)} %bitcast.132), calls=%async_computation.5 | async-start | bytes 8388608 | tf_op jit(solution)/shard_map/all_to_all | solution.py:128
  235.1 101.1 %all-to-all-done.5 = bf16[128,32,512]{2,1,0:T(8,128)(2,1)} async-done(((bf16[128,32,512]{2,1,0:T(8,128)(2,1)}), bf16[128,32,512]{2,1,0:T(8,128)(2,1)}, u32[]{:S(2)}, u32[]{:S(2)}) %all-to-all-start.5) | async-done | bytes 4194336 | tf_op jit(solution)/shard_map/all_to_all | solution.py:128
  336.2 10.3 %gather_fusion.8 = bf16[2048,512]{1,0:T(8,128)(2,1)S(1)} fusion(bf16[4096,512]{1,0:T(8,128)(2,1)} %bitcast.27, s32[2048]{0:T(1024)S(1)} %broadcast_clamp_fusion.1), kind=kCustom, calls=%fused_computation.8 | custom fusion | bytes 4202496 | tf_op jit(solution)/shard_map/gather | solution.py:129
  346.6 3.6 convolution_convert_fusion
  350.2 6.6 %convert_add_fusion = f32[2048,1024]{1,0:T(8,128)} fusion(bf16[2048,1024]{1,0:T(8,128)(2,1)S(1)} %convolution_convert_fusion, bf16[128,1024]{1,0:T(8,128)(2,1)S(1)} %copy-done.5, f32[128]{0:T(128)S(1)} %copy-done.13, f32[128]{0:T(128)S(1)} %copy-done.15, f32[2048]{0:T(1024)S(1)} %mul.102), kind=kOutput, calls=%fused_computation.19 | convolution fusion | flops 541851648 | bytes 12854272 | tf_op jit(solution)/shard_map/dot_general | solution.py:134
  356.9 13.4 %reshape.141 = f32[128,16,2,8,64]{4,3,2,1,0:T(8,128)} reshape(f32[2048,1024]{1,0:T(8,128)} %convert_add_fusion) | data formatting | bytes 16777216 | tf_op jit(solution)/shard_map/reshape | solution.py:135
  370.3 5.7 %fusion.4 = f32[128,8,16]{1,2,0:T(8,128)S(1)} fusion(f32[128,16,2,8,64]{4,3,2,1,0:T(8,128)} %reshape.141, f32[128,8,64]{2,1,0:T(8,128)S(1)} %copy-done.3), kind=kLoop, calls=%fused_computation.18 | loop fusion | flops 2080768 | bytes 4521984
  377.2 5.3 %fusion.2 = bf16[128,8,64]{2,1,0:T(8,128)(2,1)S(1)} fusion(f32[128,16,2,8,64]{4,3,2,1,0:T(8,128)} %reshape.141, f32[128,8,16]{1,2,0:T(8,128)S(1)} %copy.78), kind=kLoop, calls=%fused_computation.15 | loop fusion | flops 2031616 | bytes 4390912
  (120 shorter events, 33.1 us)
Async XLA Ops:
  7.2 75.6 %copy-start = (bf16[1152,512]{1,0:T(8,128)(2,1)S(1)}, bf16[1152,512]{1,0:T(8,128)(2,1)}, u32[]{:S(2)}) copy-start(bf16[1152,512]{1,0:T(8,128)(2,1)} %param.29) | copy-start | bytes 3538948
  7.2 31.8 %copy-start.1 = (s32[512]{0:T(512)S(1)}, s32[512]{0:T(512)}, u32[]{:S(2)}) copy-start(s32[512]{0:T(512)} %param.19) | copy-start | bytes 6148
  11.6 25.2 %all-to-all-start = ((s32[128,1,2]{2,1,0:T(1,128)}), s32[128,1,2]{2,1,0:T(1,128)S(1)}, u32[]{:S(2)}, u32[]{:S(2)}) async-start(s32[128,1,2]{2,1,0:T(1,128)} %bitcast.5), calls=%async_computation | async-start | bytes 131072 | tf_op jit(solution)/shard_map/all_to_all | solution.py:83
  39.0 13.9 %copy-start.9 = (s32[128,16]{0,1:T(8,128)S(1)}, s32[128,16]{0,1:T(8,128)}, u32[]{:S(2)}) copy-start(s32[128,16]{0,1:T(8,128)} %param.25) | copy-start | bytes 24580
  39.0 14.0 %copy-start.2 = (f32[512,512]{1,0:T(8,128)S(1)}, f32[512,512]{1,0:T(8,128)}, u32[]{:S(2)}) copy-start(f32[512,512]{1,0:T(8,128)} %param.18) | copy-start | bytes 3145732
  41.0 30.9 %copy-start.18 = (s32[128]{0:T(128)S(1)}, s32[128]{0:T(128)}, u32[]{:S(2)}) copy-start(s32[128]{0:T(128)} %param.23) | copy-start | bytes 1540
  41.0 30.9 %copy-start.12 = (f32[128]{0:T(128)S(1)}, f32[128]{0:T(128)}, u32[]{:S(2)}) copy-start(f32[128]{0:T(128)} %param.28) | copy-start | bytes 1540
  41.0 30.9 %copy-start.14 = (f32[128]{0:T(128)S(1)}, f32[128]{0:T(128)}, u32[]{:S(2)}) copy-start(f32[128]{0:T(128)} %param.27) | copy-start | bytes 1540
  41.8 17.7 %all-to-all-start.2 = ((s32[128,1,2]{2,1,0:T(1,128)}), s32[128,1,2]{2,1,0:T(1,128)S(1)}, u32[]{:S(2)}, u32[]{:S(2)}) async-start(s32[128,1,2]{2,1,0:T(1,128)} %bitcast.6), calls=%async_computation.2 | async-start | bytes 131072 | tf_op jit(solution)/shard_map/all_to_all | solution.py:89
  59.5 22.4 %all-to-all-start.1 = ((bf16[128,2,512]{2,1,0:T(2,128)(2,1)}), bf16[128,2,512]{2,1,0:T(2,128)(2,1)S(1)}, u32[]{:S(2)}, u32[]{:S(2)}) async-start(bf16[128,2,512]{2,1,0:T(2,128)(2,1)} %reshape.151), calls=%async_computation.1 | async-start | bytes 524288 | tf_op jit(solution)/shard_map/all_to_all | solution.py:88
  83.4 37.8 %copy-start.6 = (bf16[256,512]{1,0:T(8,128)(2,1)}, bf16[256,512]{1,0:T(8,128)(2,1)S(1)}, u32[]{:S(2)}) copy-start(bf16[256,512]{1,0:T(8,128)(2,1)S(1)} %multiply_convert_fusion) | copy-start | bytes 786436
  83.4 38.3 %copy-start.16 = (s32[128]{0:T(128)S(1)}, s32[128]{0:T(128)}, u32[]{:S(2)}) copy-start(s32[128]{0:T(128)} %param.20) | copy-start | bytes 1540
  85.4 38.6 %copy-start.17 = (f32[4,128]{1,0:T(4,128)S(1)}, f32[4,128]{1,0:T(4,128)}, u32[]{:S(2)}) copy-start(f32[4,128]{1,0:T(4,128)} %param.32) | copy-start | bytes 6148
  85.4 21.6 %all-to-all-start.3 = ((bf16[128,2,512]{2,1,0:T(2,128)(2,1)}), bf16[128,2,512]{2,1,0:T(2,128)(2,1)S(1)}, u32[]{:S(2)}, u32[]{:S(2)}) async-start(bf16[128,2,512]{2,1,0:T(2,128)(2,1)} %reshape.135), calls=%async_computation.3 | async-start | bytes 524288 | tf_op jit(solution)/shard_map/all_to_all | solution.py:102
  94.3 8.1 %copy-start.7 = (s32[2048,1]{0,1:T(1,128)}, s32[2048,1]{0,1:T(1,128)S(1)}, u32[]{:S(2)}) copy-start(s32[2048,1]{0,1:T(1,128)S(1)} %compare_select_fusion) | copy-start | bytes 24580
  107.0 26.0 %all-to-all-start.4 = ((s32[128,1,32]{2,1,0:T(1,128)}), s32[128,1,32]{2,1,0:T(1,128)}, u32[]{:S(2)}, u32[]{:S(2)}) async-start(s32[128,1,32]{2,1,0:T(1,128)} %bitcast.135), calls=%async_computation.4 | async-start | bytes 131072 | tf_op jit(solution)/shard_map/all_to_all | solution.py:84
  121.3 58.9 %all-reduce.2.cloned.1.call-start = ((), (), s32[]{:S(2)}) async-start(), calls=%async_computation.6 | async-start | bytes 2097152 | tf_op jit(solution)/shard_map/psum | solution.py:113
  213.3 19.2 %copy-start.19 = (s32[128]{0:T(128)S(1)}, s32[128]{0:T(128)}, u32[]{:S(2)}) copy-start(s32[128]{0:T(128)} %param.23) | copy-start | bytes 1540
  213.3 19.2 %copy-start.10 = (s32[128,16]{0,1:T(8,128)S(1)}, s32[128,16]{0,1:T(8,128)}, u32[]{:S(2)}) copy-start(s32[128,16]{0,1:T(8,128)} %param.26) | copy-start | bytes 24580
  213.3 19.5 %copy-start.8 = (s32[2048,1]{0,1:T(1,128)S(1)}, s32[2048,1]{0,1:T(1,128)}, u32[]{:S(2)}) copy-start(s32[2048,1]{0,1:T(1,128)} %copy-done.7) | copy-start | bytes 24580
  213.3 20.4 %copy-start.4 = (bf16[512,512]{1,0:T(8,128)(2,1)S(1)}, bf16[512,512]{1,0:T(8,128)(2,1)}, u32[]{:S(2)}) copy-start(bf16[512,512]{1,0:T(8,128)(2,1)} %param.33) | copy-start | bytes 1572868
  213.3 122.9 %all-to-all-start.5 = ((bf16[128,32,512]{2,1,0:T(8,128)(2,1)}), bf16[128,32,512]{2,1,0:T(8,128)(2,1)}, u32[]{:S(2)}, u32[]{:S(2)}) async-start(bf16[128,32,512]{2,1,0:T(8,128)(2,1)} %bitcast.132), calls=%async_computation.5 | async-start | bytes 8388608 | tf_op jit(solution)/shard_map/all_to_all | solution.py:128
  346.6 3.6 copy-start.5
  356.8 13.4 %copy-start.3 = (f32[128,8,64]{2,1,0:T(8,128)S(1)}, f32[128,8,64]{2,1,0:T(8,128)}, u32[]{:S(2)}) copy-start(f32[128,8,64]{2,1,0:T(8,128)} %copy.77) | copy-start | bytes 786436
  (3 other events, 9.0 us)
Sparse Core Ops, SparseCore 0:
  124.4 55.7 all-reduce.1
where the time goes:
time: 392 us; the launch traced here: 390 us
  waiting for transfers between devices  164 us (42%)
  starting transfers between devices  79.3 us (20%)
  local copies, waits for them, and re-layouts  70.6 us (18%)
  other arithmetic  21.3 us (5%)
  blocking collectives  20.3 us (5%)
  matrix products  19.8 us (5%)
  between operations  14.7 us (4%)
    all_to_all x1, waiting for transfers between devices, on_device(): lax.all_to_all(served, 'nodes', split_axis=0, concat_axis=0, tiled=True)  101 us
    psum x1, waiting for transfers between devices, on_device(): sums, counts = lax.psum((sums, counts), 'rep')  46.1 us
    all_to_all x1, starting transfers between devices, on_device(): lax.all_to_all(served, 'nodes', split_axis=0, concat_axis=0, tiled=True)  19.2 us
    gather x1, local copies, waits for them, and re-layouts, on_device(): served = updated[jnp.maximum(got_nbr, 0)]  17.3 us
    all_to_all x1, starting transfers between devices, on_device(): lax.all_to_all(dst_ids, 'nodes', split_axis=0, concat_axis=0, tiled=True)  17.2 us
    all_to_all x1, starting transfers between devices, on_device(): lax.all_to_all(nbr_ids, 'nodes', split_axis=0, concat_axis=0, tiled=True)  14.2 us
    reshape x1, local copies, waits for them, and re-layouts, on_device(): keyval = (kv_mem + kv_time).reshape(events, neighbours, 2, HEADS, HEAD_DIM)  13.4 us
    all_gather x1, blocking collectives, on_device(): lax.all_gather(new_part.astype(jnp.bfloat16), 'rep', axis=1, tiled=True)  11.5 us
  transfers between devices with their start and end apart: 7, of which 5 were waited for; matrix products, arithmetic and copies ran while one was open for 8% of the time, Pallas kernels for 0%

commit v1 on v0

--- a/solution.py
+++ b/solution.py
@@ -6,6 +6,16 @@
 
 HEADS = 8
 HEAD_DIM = 64
+
+
+def _cover_pairs_all(values, axis_k):
+    spare = jnp.concatenate(
+        jax.lax.all_to_all(
+            jnp.stack([values] * jax.lax.axis_size("rep")), "rep", split_axis=0, concat_axis=0
+        ),
+        axis=axis_k,
+    )
+    return spare
 
 
 def encode(gaps, freq, phase):
@@ -123,7 +133,7 @@
     cand = jnp.tanh(a_parts[2] + gru_bias[2] + reset * (b_parts[2] + gru_bias[3]))
     fresh = (1.0 - update) * cand + update * state_part
     new_part = jnp.where((counts > 0.0)[:, None], fresh, state_part)
-    updated = lax.all_gather(new_part.astype(jnp.bfloat16), "rep", axis=1, tiled=True)
+    updated = _cover_pairs_all(new_part.astype(jnp.bfloat16), axis_k=1)
     served = updated[jnp.maximum(got_nbr, 0)]
     returned = lax.all_to_all(served, "nodes", split_axis=0, concat_axis=0, tiled=True)
     fetched = returned.reshape(-1, updated.shape[1])[nbr_slot]

time: 392 us -> 386 us (0.985)
  blocking collectives: 20.3 us -> 8.71 us
  waiting for transfers between devices: 164 us -> 173 us
    all_gather x1 -> x0, blocking collectives: 11.5 us -> none  [on_device(): lax.all_gather(new_part.astype(jnp.bfloat16), 'rep', axis=1, tiled=True)]
    all_to_all x0 -> x1, waiting for transfers between devices: none -> 6.6 us  [_cover_pairs_all(): jax.lax.all_to_all(jnp.stack([values] * jax.lax.axis_size('rep')), 'rep',...]
  transfers between devices with their start and end apart: 7 -> 8, of which waited for: 5 -> 7; matrix products, arithmetic and copies ran while one was open for 8% -> 8% of each run, Pallas kernels for 0% -> 0%
where the time goes in v1:
time: 386 us; the launch traced here: 384 us
  waiting for transfers between devices  173 us (45%)
  starting transfers between devices  78.3 us (20%)
  local copies, waits for them, and re-layouts  70.6 us (18%)
  other arithmetic  20.1 us (5%)
  matrix products  18.9 us (5%)
  between operations  14.6 us (4%)
  blocking collectives  8.71 us (2%)
    all_to_all x1, waiting for transfers between devices, on_device(): lax.all_to_all(served, 'nodes', split_axis=0, concat_axis=0, tiled=True)  101 us
    psum x1, waiting for transfers between devices, on_device(): sums, counts = lax.psum((sums, counts), 'rep')  45.2 us
    all_to_all x1, starting transfers between devices, on_device(): lax.all_to_all(served, 'nodes', split_axis=0, concat_axis=0, tiled=True)  18.4 us
    gather x1, local copies, waits for them, and re-layouts, on_device(): served = updated[jnp.maximum(got_nbr, 0)]  17.3 us
    all_to_all x1, starting transfers between devices, on_device(): lax.all_to_all(dst_ids, 'nodes', split_axis=0, concat_axis=0, tiled=True)  17.2 us
    reshape x1, local copies, waits for them, and re-layouts, on_device(): keyval = (kv_mem + kv_time).reshape(events, neighbours, 2, HEADS, HEAD_DIM)  13.4 us
    unnamed x2, other arithmetic  10.9 us
    all_to_all x1, starting transfers between devices, on_device(): lax.all_to_all(nbr_ids, 'nodes', split_axis=0, concat_axis=0, tiled=True)  10.7 us
  transfers between devices with their start and end apart: 8, of which 7 were waited for; matrix products, arithmetic and copies ran while one was open for 8% of the time, Pallas kernels for 0%

profile of v1, /device:TPU:41, one launch (start us, length us, event | category | flops | bytes accessed | tf_op | source)
XLA Modules:
  0.0 384.4 jit_solution(16366311658961566390)
XLA Ops:
  11.6 17.2 %all-to-all-start = ((s32[128,1,2]{2,1,0:T(1,128)}), s32[128,1,2]{2,1,0:T(1,128)S(1)}, u32[]{:S(2)}, u32[]{:S(2)}) async-start(s32[128,1,2]{2,1,0:T(1,128)} %bitcast.5), calls=%async_computation | async-start | bytes 131072 | tf_op jit(solution)/shard_map/all_to_all | solution.py:93
  32.7 4.2 %all-to-all-done = s32[128,1,2]{2,1,0:T(1,128)S(1)} async-done(((s32[128,1,2]{2,1,0:T(1,128)}), s32[128,1,2]{2,1,0:T(1,128)S(1)}, u32[]{:S(2)}, u32[]{:S(2)}) %all-to-all-start) | async-done | bytes 1056 | tf_op jit(solution)/shard_map/all_to_all | solution.py:93
  41.4 9.6 %all-to-all-start.2 = ((s32[128,1,2]{2,1,0:T(1,128)}), s32[128,1,2]{2,1,0:T(1,128)S(1)}, u32[]{:S(2)}, u32[]{:S(2)}) async-start(s32[128,1,2]{2,1,0:T(1,128)} %bitcast.6), calls=%async_computation.2 | async-start | bytes 131072 | tf_op jit(solution)/shard_map/all_to_all | solution.py:99
  55.6 3.5 all-to-all-done.2
  59.0 10.3 %all-to-all-start.1 = ((bf16[128,2,512]{2,1,0:T(2,128)(2,1)}), bf16[128,2,512]{2,1,0:T(2,128)(2,1)S(1)}, u32[]{:S(2)}, u32[]{:S(2)}) async-start(bf16[128,2,512]{2,1,0:T(2,128)(2,1)} %reshape.161), calls=%async_computation.1 | async-start | bytes 524288 | tf_op jit(solution)/shard_map/all_to_all | solution.py:98
  72.2 9.3 %all-to-all-done.1 = bf16[128,2,512]{2,1,0:T(2,128)(2,1)S(1)} async-done(((bf16[128,2,512]{2,1,0:T(2,128)(2,1)}), bf16[128,2,512]{2,1,0:T(2,128)(2,1)S(1)}, u32[]{:S(2)}, u32[]{:S(2)}) %all-to-all-start.1) | async-done | bytes 262176 | tf_op jit(solution)/shard_map/all_to_all | solution.py:98
  85.0 8.7 %all-to-all-start.3 = ((bf16[128,2,512]{2,1,0:T(2,128)(2,1)}), bf16[128,2,512]{2,1,0:T(2,128)(2,1)S(1)}, u32[]{:S(2)}, u32[]{:S(2)}) async-start(bf16[128,2,512]{2,1,0:T(2,128)(2,1)} %reshape.143), calls=%async_computation.3 | async-start | bytes 524288 | tf_op jit(solution)/shard_map/all_to_all | solution.py:112
  93.7 8.1 %scatter_custom_fusion.2 = s32[4096]{0:T(1024)S(1)} fusion(s32[2048]{0:T(1024)S(1)} %bitcast.142, s32[2048]{0:T(1024)S(1)} %reshape.244, s32[]{:T(128)} %constant.15.clone.1), kind=kCustom, calls=%fused_computation.110 | custom fusion | bytes 16388 | tf_op jit(solution)/shard_map/scatter | solution.py:85
  102.7 3.1 all-to-all-done.3
  105.9 10.7 %all-to-all-start.5 = ((s32[128,1,32]{2,1,0:T(1,128)}), s32[128,1,32]{2,1,0:T(1,128)S(1)}, u32[]{:S(2)}, u32[]{:S(2)}) async-start(s32[128,1,32]{2,1,0:T(1,128)} %bitcast.26), calls=%async_computation.5 | async-start | bytes 131072 | tf_op jit(solution)/shard_map/all_to_all | solution.py:94
  121.5 8.7 %psum.14 = f32[512]{0:T(512)S(1)} all-reduce(f32[512]{0:T(512)S(1)} %add.150), channel_id=1, replica_groups=mesh['nodes'=128,'rep'=4] {'rep'}, use_global_device_ids=true, to_apply=%region_5.6 | all-reduce | flops 512 | bytes 4096 | tf_op jit(solution)/shard_map/psum | solution.py:123
  130.2 45.2 %all-reduce.2.cloned.1.call-done = f32[512,512]{1,0:T(8,128)} async-done(((f32[512,512]{1,0:T(8,128)}), f32[512,512]{1,0:T(8,128)}) %all-reduce.2.cloned.1.call-update) | async-done | bytes 1048592 | tf_op jit(solution)/shard_map/psum | solution.py:123
  175.4 3.3 convolution_bitcast_fusion.1
  180.5 3.5 all-to-all-start.4
  184.3 6.6 %all-to-all-done.4 = bf16[4,512,128]{2,1,0:T(8,128)(2,1)S(1)} async-done(((bf16[4,512,128]{2,1,0:T(8,128)(2,1)}), bf16[4,512,128]{2,1,0:T(8,128)(2,1)S(1)}, u32[]{:S(2)}, u32[]{:S(2)}) %all-to-all-start.4) | async-done | bytes 524320 | tf_op jit(solution)/shard_map/all_to_all | solution.py:13
  191.0 17.3 %gather_fusion.7 = bf16[4096,512]{1,0:T(8,128)(2,1)} fusion(bf16[512,512]{1,0:T(8,128)(2,1)S(1)} %copy_bitcast_fusion, s32[4096]{0:T(1024)S(1)} %broadcast_clamp_fusion), kind=kCustom, calls=%fused_computation.7 | custom fusion | bytes 8404992 | tf_op jit(solution)/shard_map/gather | solution.py:137
  208.3 18.4 %all-to-all-start.6 = ((bf16[128,32,512]{2,1,0:T(8,128)(2,1)}), bf16[128,32,512]{2,1,0:T(8,128)(2,1)}, u32[]{:S(2)}, u32[]{:S(2)}) async-start(bf16[128,32,512]{2,1,0:T(8,128)(2,1)} %bitcast.138), calls=%async_computation.6 | async-start | bytes 8388608 | tf_op jit(solution)/shard_map/all_to_all | solution.py:138
  229.1 101.3 %all-to-all-done.6 = bf16[128,32,512]{2,1,0:T(8,128)(2,1)} async-done(((bf16[128,32,512]{2,1,0:T(8,128)(2,1)}), bf16[128,32,512]{2,1,0:T(8,128)(2,1)}, u32[]{:S(2)}, u32[]{:S(2)}) %all-to-all-start.6) | async-done | bytes 4194336 | tf_op jit(solution)/shard_map/all_to_all | solution.py:138
  330.4 10.3 %gather_fusion.8 = bf16[2048,512]{1,0:T(8,128)(2,1)S(1)} fusion(bf16[4096,512]{1,0:T(8,128)(2,1)} %bitcast.28, s32[2048]{0:T(1024)S(1)} %broadcast_clamp_fusion.1), kind=kCustom, calls=%fused_computation.8 | custom fusion | bytes 4202496 | tf_op jit(solution)/shard_map/gather | solution.py:139
  340.7 3.6 convolution_convert_fusion
  344.3 6.6 %convert_add_fusion = f32[2048,1024]{1,0:T(8,128)} fusion(bf16[2048,1024]{1,0:T(8,128)(2,1)S(1)} %convolution_convert_fusion, bf16[128,1024]{1,0:T(8,128)(2,1)S(1)} %copy-done.5, f32[128]{0:T(128)S(1)} %copy-done.8, f32[128]{0:T(128)S(1)} %copy-done.9, f32[2048]{0:T(1024)S(1)} %mul.102), kind=kOutput, calls=%fused_computation.19 | convolution fusion | flops 541851648 | bytes 12854272 | tf_op jit(solution)/shard_map/dot_general | solution.py:144
  351.0 13.4 %reshape.151 = f32[128,16,2,8,64]{4,3,2,1,0:T(8,128)} reshape(f32[2048,1024]{1,0:T(8,128)} %convert_add_fusion) | data formatting | bytes 16777216 | tf_op jit(solution)/shard_map/reshape | solution.py:145
  364.4 5.7 %fusion.4 = f32[128,8,16]{1,2,0:T(8,128)S(1)} fusion(f32[128,16,2,8,64]{4,3,2,1,0:T(8,128)} %reshape.151, f32[128,8,64]{2,1,0:T(8,128)S(1)} %copy-done.3), kind=kLoop, calls=%fused_computation.18 | loop fusion | flops 2080768 | bytes 4521984
  371.3 5.3 %fusion.2 = bf16[128,8,64]{2,1,0:T(8,128)(2,1)S(1)} fusion(f32[128,16,2,8,64]{4,3,2,1,0:T(8,128)} %reshape.151, f32[128,8,16]{1,2,0:T(8,128)S(1)} %copy.80), kind=kLoop, calls=%fused_computation.15 | loop fusion | flops 2031616 | bytes 4390912
  (109 shorter events, 36.1 us)
Async XLA Ops:
  7.2 75.2 %copy-start = (bf16[1152,512]{1,0:T(8,128)(2,1)S(1)}, bf16[1152,512]{1,0:T(8,128)(2,1)}, u32[]{:S(2)}) copy-start(bf16[1152,512]{1,0:T(8,128)(2,1)} %param.29) | copy-start | bytes 3538948
  7.2 31.4 %copy-start.1 = (s32[512]{0:T(512)S(1)}, s32[512]{0:T(512)}, u32[]{:S(2)}) copy-start(s32[512]{0:T(512)} %param.19) | copy-start | bytes 6148
  11.6 25.2 %all-to-all-start = ((s32[128,1,2]{2,1,0:T(1,128)}), s32[128,1,2]{2,1,0:T(1,128)S(1)}, u32[]{:S(2)}, u32[]{:S(2)}) async-start(s32[128,1,2]{2,1,0:T(1,128)} %bitcast.5), calls=%async_computation | async-start | bytes 131072 | tf_op jit(solution)/shard_map/all_to_all | solution.py:93
  38.6 13.9 %copy-start.6 = (s32[128,16]{0,1:T(8,128)S(1)}, s32[128,16]{0,1:T(8,128)}, u32[]{:S(2)}) copy-start(s32[128,16]{0,1:T(8,128)} %param.25) | copy-start | bytes 24580
  38.6 14.0 %copy-start.2 = (f32[512,512]{1,0:T(8,128)S(1)}, f32[512,512]{1,0:T(8,128)}, u32[]{:S(2)}) copy-start(f32[512,512]{1,0:T(8,128)} %param.18) | copy-start | bytes 3145732
  40.6 31.0 %copy-start.12 = (s32[128]{0:T(128)S(1)}, s32[128]{0:T(128)}, u32[]{:S(2)}) copy-start(s32[128]{0:T(128)} %param.23) | copy-start | bytes 1540
  40.6 31.0 %copy-start.8 = (f32[128]{0:T(128)S(1)}, f32[128]{0:T(128)}, u32[]{:S(2)}) copy-start(f32[128]{0:T(128)} %param.28) | copy-start | bytes 1540
  40.6 31.0 %copy-start.9 = (f32[128]{0:T(128)S(1)}, f32[128]{0:T(128)}, u32[]{:S(2)}) copy-start(f32[128]{0:T(128)} %param.27) | copy-start | bytes 1540
  41.4 17.6 %all-to-all-start.2 = ((s32[128,1,2]{2,1,0:T(1,128)}), s32[128,1,2]{2,1,0:T(1,128)S(1)}, u32[]{:S(2)}, u32[]{:S(2)}) async-start(s32[128,1,2]{2,1,0:T(1,128)} %bitcast.6), calls=%async_computation.2 | async-start | bytes 131072 | tf_op jit(solution)/shard_map/all_to_all | solution.py:99
  59.0 22.4 %all-to-all-start.1 = ((bf16[128,2,512]{2,1,0:T(2,128)(2,1)}), bf16[128,2,512]{2,1,0:T(2,128)(2,1)S(1)}, u32[]{:S(2)}, u32[]{:S(2)}) async-start(bf16[128,2,512]{2,1,0:T(2,128)(2,1)} %reshape.161), calls=%async_computation.1 | async-start | bytes 524288 | tf_op jit(solution)/shard_map/all_to_all | solution.py:98
  82.4 20.1 %copy-start.10 = (s32[128]{0:T(128)S(1)}, s32[128]{0:T(128)}, u32[]{:S(2)}) copy-start(s32[128]{0:T(128)} %param.20) | copy-start | bytes 1540
  83.0 35.4 %copy-start.11 = (f32[4,128]{1,0:T(4,128)S(1)}, f32[4,128]{1,0:T(4,128)}, u32[]{:S(2)}) copy-start(f32[4,128]{1,0:T(4,128)} %param.32) | copy-start | bytes 6148
  85.0 20.9 %all-to-all-start.3 = ((bf16[128,2,512]{2,1,0:T(2,128)(2,1)}), bf16[128,2,512]{2,1,0:T(2,128)(2,1)S(1)}, u32[]{:S(2)}, u32[]{:S(2)}) async-start(bf16[128,2,512]{2,1,0:T(2,128)(2,1)} %reshape.143), calls=%async_computation.3 | async-start | bytes 524288 | tf_op jit(solution)/shard_map/all_to_all | solution.py:112
  105.9 73.8 %all-to-all-start.5 = ((s32[128,1,32]{2,1,0:T(1,128)}), s32[128,1,32]{2,1,0:T(1,128)S(1)}, u32[]{:S(2)}, u32[]{:S(2)}) async-start(s32[128,1,32]{2,1,0:T(1,128)} %bitcast.26), calls=%async_computation.5 | async-start | bytes 131072 | tf_op jit(solution)/shard_map/all_to_all | solution.py:94
  116.6 58.9 %all-reduce.2.cloned.1.call-start = ((), (), s32[]{:S(2)}) async-start(), calls=%async_computation.7 | async-start | bytes 2097152 | tf_op jit(solution)/shard_map/psum | solution.py:123
  180.5 10.4 %all-to-all-start.4 = ((bf16[4,512,128]{2,1,0:T(8,128)(2,1)}), bf16[4,512,128]{2,1,0:T(8,128)(2,1)S(1)}, u32[]{:S(2)}, u32[]{:S(2)}) async-start(bf16[4,512,128]{2,1,0:T(8,128)(2,1)} %stack.2), calls=%async_computation.4 | async-start | bytes 1048576 | tf_op jit(solution)/shard_map/all_to_all | solution.py:13
  208.3 18.4 %copy-start.7 = (s32[128,16]{0,1:T(8,128)S(1)}, s32[128,16]{0,1:T(8,128)}, u32[]{:S(2)}) copy-start(s32[128,16]{0,1:T(8,128)} %param.26) | copy-start | bytes 24580
  208.3 19.5 %copy-start.4 = (bf16[512,512]{1,0:T(8,128)(2,1)S(1)}, bf16[512,512]{1,0:T(8,128)(2,1)}, u32[]{:S(2)}) copy-start(bf16[512,512]{1,0:T(8,128)(2,1)} %param.33) | copy-start | bytes 1572868
  208.3 122.1 %all-to-all-start.6 = ((bf16[128,32,512]{2,1,0:T(8,128)(2,1)}), bf16[128,32,512]{2,1,0:T(8,128)(2,1)}, u32[]{:S(2)}, u32[]{:S(2)}) async-start(bf16[128,32,512]{2,1,0:T(8,128)(2,1)} %bitcast.138), calls=%async_computation.6 | async-start | bytes 8388608 | tf_op jit(solution)/shard_map/all_to_all | solution.py:138
  340.7 3.6 copy-start.5
  351.0 13.4 %copy-start.3 = (f32[128,8,64]{2,1,0:T(8,128)S(1)}, f32[128,8,64]{2,1,0:T(8,128)}, u32[]{:S(2)}) copy-start(f32[128,8,64]{2,1,0:T(8,128)} %copy.79) | copy-start | bytes 786436
Sparse Core Ops, SparseCore 0:
  119.7 55.6 all-reduce.1
